TPU v7x, 512 devices: a whole 4x8x8 slice. The times are simulated.
512 devices in a mesh: req: 64 (over z, x, core), tp: 8 (over y).
Axes of the slice: x: 4, y: 8, z: 8, core: 2. Of those that a mesh axis runs over, the one named last changes fastest.
Arguments:
- queries: bfloat16 [16384, 7168], P('req', 'tp'), may hold values from -200 to 200
- key_value: bfloat16 [2, 16384, 1024], P(None, 'req', 'tp'), may hold values from -8 to 8
- segment: int32 [16384], P('req'), may hold values from 0 to 31, never falling along the last dimension, each value on 1 to 1024 neighbouring positions
- residual: bfloat16 [16384, 7168], P('req', 'tp'), may hold values from -4 to 4
- out_weight: bfloat16 [7168, 7168], P('tp', 'req'), may hold values from -0.0625 to 0.0625
- head_gain: bfloat16 [7168], P('tp'), may hold values from 0.099609375 to 1.8984375
- vocab_weight: bfloat16 [7168, 64000], P('tp', 'req'), may hold values from -0.21875 to 0.21875
Outputs:
- hidden: bfloat16 [16384, 7168], P('req', 'tp')
- key_cache: bfloat16 [16384, 1024], P('req', 'tp')
- last_norm: float32 [32], replicated
- top_logit: float32 [32], replicated
Inputs may be any that keep to these rules, and one draw needn't show every extreme that they name: `segment`: ids never fall; each of the 32 requests has 1 to 1024 tokens, one has exactly 1024.
All inputs are finite; a program needn't handle non-finite values.
Results may differ from a plain program's by a relative error of at most 0.013.
Values may be sent and summed in bfloat16 or wider, within the bound.
No kernel may reach another device: no remote copies, remote signals or barrier semaphores. Data moves between devices by JAX's collectives and lax.ppermute only.
A program may use at most 128 MiB of HBM per device.

v0:
```python
import jax
import jax.numpy as jnp
from jax import lax
from jax.sharding import PartitionSpec as P

D = 7168
HD = 128
GROUP = 7
REACH = 4
theta = 5000000.0
eps = 1e-05
masked_score = -1e30


def from_behind(value, axis, steps):
    count = lax.axis_size(axis)
    initial, last = (max(0, -steps), min(count, count - steps))
    return lax.ppermute(value, axis, [(source, source + steps) for source in range(initial, last)])


def butterfly(value, axis, combine):
    count = lax.axis_size(axis)
    stride = 1
    while stride < count:
        other = lax.ppermute(value, axis, [(source, source ^ stride) for source in range(count)])
        value = combine(value, other)
        stride *= 2
    return value


def halving_scatter(value, axis):
    count = lax.axis_size(axis)
    index = lax.axis_index(axis)
    rows, width = (value.shape[1], value.shape[2])
    held = jnp.moveaxis(value, 0, 1)
    bit = 1
    while bit < count:
        mine = index // bit % 2
        pairs = held.reshape(rows, held.shape[1] // 2, 2, width)
        keep = lax.dynamic_index_in_dim(pairs, mine, 2, keepdims=False)
        give = lax.dynamic_index_in_dim(pairs, 1 - mine, 2, keepdims=False)
        moved = lax.ppermute(give, axis, [(source, source ^ bit) for source in range(count)])
        held = (keep.astype(jnp.float32) + moved.astype(jnp.float32)).astype(value.dtype)
        bit *= 2
    return held.reshape(rows, width).astype(jnp.float32)


def rope_tables(positions, width):
    half_width = width // 2
    frequency = theta ** (-(jnp.arange(half_width, dtype=jnp.float32) * 2.0 / width))
    angles = positions[:, None] * frequency[None, :]
    return (jnp.cos(angles), jnp.sin(angles))


def rotate(values, cosine, sine_table):
    half_width = values.shape[-1] // 2
    first_half = values[..., :half_width]
    second_half = values[..., half_width:]
    table_shape = (cosine.shape[0],) + (1,) * (values.ndim - 2) + (half_width,)
    cosine = cosine.reshape(table_shape)
    sine_table = sine_table.reshape(table_shape)
    return jnp.concatenate(
        [
            first_half * cosine - second_half * sine_table,
            second_half * cosine + first_half * sine_table,
        ],
        axis=-1,
    )


def local(queries, key_value, segment, residual, out_weight, head_gain, vocab_weight):
    tok_rows = segment.shape[0]
    heads_kv = key_value.shape[2] // HD
    requests = lax.axis_size("req") // 2
    devices_req = lax.axis_size("req")
    device = lax.axis_index("req")
    request_ids = jnp.arange(requests, dtype=jnp.int32)
    own_kv = key_value
    width = own_kv.shape[2]
    seg_rows = -(-tok_rows // width)
    seg_flat = jnp.pad(segment, (0, seg_rows * width - tok_rows)).astype(jnp.bfloat16)
    packed = jnp.concatenate(
        [own_kv.reshape(2 * tok_rows, width), seg_flat.reshape(seg_rows, width)], axis=0
    )
    parts_kv, parts_seg = ([], [])
    for back in range(REACH, 0, -1):
        got = from_behind(packed, "req", back)
        parts_kv.append(got[: 2 * tok_rows].reshape(own_kv.shape))
        parts_seg.append(got[2 * tok_rows :].reshape(-1)[:tok_rows].astype(jnp.int32))
    parts_kv.append(own_kv)
    parts_seg.append(segment)
    window = jnp.concatenate(parts_kv, axis=1)
    seg_window = jnp.concatenate(parts_seg, axis=0)
    span = window.shape[1]
    key_index_i = (device - REACH) * tok_rows + jnp.arange(span, dtype=jnp.int32)
    valid = key_index_i >= 0
    same = (seg_window[:, None] == seg_window[None, :]) & valid[None, :]
    start_i = jnp.min(jnp.where(same, key_index_i[None, :], jnp.int32(2**30)), axis=1)
    key_index = key_index_i.astype(jnp.float32)
    win_start = start_i.astype(jnp.float32)
    win_pos = key_index - win_start
    own_start = win_start[span - tok_rows :]
    tok_index = key_index[span - tok_rows :]
    positions = win_pos[span - tok_rows :]
    cosine, sine_table = rope_tables(win_pos, HD)
    rot_keys = rotate(
        window[0].astype(jnp.float32).reshape(span, heads_kv, HD), cosine, sine_table
    ).astype(jnp.bfloat16)
    q_cos, q_sin = (cosine[span - tok_rows :], sine_table[span - tok_rows :])
    rot_query = rotate(
        queries.astype(jnp.float32).reshape(tok_rows, heads_kv, GROUP, HD), q_cos, q_sin
    ).astype(jnp.bfloat16)
    key_cache = rot_keys[span - tok_rows :].reshape(tok_rows, heads_kv * HD)
    key_rows = rot_keys
    value_rows = window[1].reshape(span, heads_kv, HD)
    q_seg = segment
    allowed = (
        (seg_window[None, :] == q_seg[:, None])
        & valid[None, :]
        & (key_index[None, :] <= tok_index[:, None])
    )
    scale = HD ** (-0.5)
    scores_part = (
        jnp.einsum("qhgd,khd->hgqk", rot_query, key_rows, preferred_element_type=jnp.float32)
        * scale
    )
    scores = jnp.where(allowed[None, None], scores_part, masked_score)
    peak = jnp.max(scores, axis=3, keepdims=True)
    weights = jnp.exp(scores - peak)
    total = jnp.sum(weights, axis=3)
    context = jnp.einsum(
        "hgqk,khd->qhgd",
        weights.astype(jnp.bfloat16),
        value_rows,
        preferred_element_type=jnp.float32,
    )
    context = context / jnp.transpose(total, (2, 0, 1))[..., None]
    attended = context.astype(jnp.bfloat16).reshape(tok_rows, heads_kv * GROUP * HD)
    is_end = jnp.concatenate([segment[1:] != segment[:-1], jnp.ones((1,), bool)])
    select = (is_end[:, None] & (segment[:, None] == request_ids[None, :])).astype(jnp.bfloat16)
    held = jnp.any(segment[:, None] == request_ids[None, :], axis=0)
    tag = jnp.where(held, device, -1).astype(jnp.bfloat16)
    end_rows = lax.dot_general(
        select,
        jnp.concatenate([attended, residual], axis=1),
        (((0,), (0,)), ((), ())),
        preferred_element_type=jnp.float32,
    ).astype(jnp.bfloat16)
    end_rows = jnp.concatenate([end_rows, tag[:, None]], axis=1)

    def latest(mine, other):
        return jnp.where(other[:, -1:] > mine[:, -1:], other, mine)

    end_rows = butterfly(end_rows, "req", latest)[:, :-1]
    attended, end_rows = lax.optimization_barrier((attended, end_rows))
    end_att, end_res = (end_rows[:, : attended.shape[1]], end_rows[:, attended.shape[1] :])
    full_weight = lax.all_gather(out_weight, "req", axis=1, tiled=True)
    groups = lax.axis_size("tp")
    both = jnp.einsum(
        "tk,kgn->gtn",
        jnp.concatenate([attended, end_att], axis=0),
        full_weight.reshape(full_weight.shape[0], groups, -1),
        preferred_element_type=jnp.float32,
    ).astype(jnp.bfloat16)
    end_part = both[:, tok_rows:]
    end_sum = halving_scatter(end_part, "tp")
    both, end_sum = lax.optimization_barrier((both, end_sum))
    own_share = lax.psum_scatter(both, "tp", scatter_dimension=0, tiled=True)[0, :tok_rows]
    own_share = own_share.astype(jnp.float32)
    hidden = (residual.astype(jnp.float32) + own_share).astype(jnp.bfloat16)
    last_state = (end_res.astype(jnp.float32) + end_sum).astype(jnp.bfloat16).astype(jnp.float32)
    scaled = (last_state * head_gain.astype(jnp.float32)).astype(jnp.bfloat16)
    square_part = jnp.sum(last_state * last_state, axis=1)
    logit_part = jnp.dot(scaled, vocab_weight, preferred_element_type=jnp.float32)
    summed = butterfly(
        jnp.concatenate([logit_part, square_part[:, None]], axis=1).astype(jnp.bfloat16),
        "tp",
        jnp.add,
    ).astype(jnp.float32)
    raw_logits, square_sum = (summed[:, :-1], summed[:, -1])
    mean_square = square_sum / D
    last_norm = jnp.sqrt(mean_square)
    local_top = jnp.max(raw_logits * lax.rsqrt(mean_square + eps)[:, None], axis=1)
    top_logit = butterfly(local_top, "req", jnp.maximum)
    return (hidden, key_cache, last_norm, top_logit)


def solution(mesh):
    placed = (
        P("req", "tp"),
        P(None, "req", "tp"),
        P("req"),
        P("req", "tp"),
        P("tp", "req"),
        P("tp"),
        P("tp", "req"),
    )
    return jax.shard_map(
        local,
        mesh=mesh,
        in_specs=placed,
        out_specs=(P("req", "tp"), P("req", "tp"), P(), P()),
        check_vma=False,
    )
```

profile of v0, /device:TPU:56, one launch (start us, length us, event | category | flops | bytes accessed | tf_op | source)
XLA Modules:
  0.0 238.6 jit_solution(11665168954545086751)
XLA Ops:
  8.7 0.9 pad_maximum_fusion
  9.6 4.9 %collective-permute-start = (bf16[514,128]{1,0:T(8,128)(2,1)S(1)}, bf16[514,128]{1,0:T(8,128)(2,1)S(1)}, u32[]{:S(2)}, u32[]{:S(2)}) collective-permute-start(bf16[514,128]{1,0:T(8,128)(2,1)S(1)} %pad_maximum_fusion), channel_id=1, source_target_pairs={{0,32},{8,40},{16,48},{24,56},{32,64},{40,72},{48,80},{56,88},{64,... | collective-permute-start | bytes 394760 | tf_op jit(solution)/shard_map/ppermute | solution.py:18
  14.5 2.3 collective-permute-start.1
  16.8 4.2 %collective-permute-start.2 = (bf16[514,128]{1,0:T(8,128)(2,1)S(1)}, bf16[514,128]{1,0:T(8,128)(2,1)}, u32[]{:S(2)}, u32[]{:S(2)}) collective-permute-start(bf16[514,128]{1,0:T(8,128)(2,1)S(1)} %pad_maximum_fusion), channel_id=1, source_target_pairs={{0,16},{8,24},{16,32},{24,40},{32,48},{40,56},{48,64},{56,72},{64,... | collective-permute-start | bytes 394760 | tf_op jit(solution)/shard_map/ppermute | solution.py:18
  21.1 4.1 %collective-permute-start.3 = (bf16[514,128]{1,0:T(8,128)(2,1)S(1)}, bf16[514,128]{1,0:T(8,128)(2,1)}, u32[]{:S(2)}, u32[]{:S(2)}) collective-permute-start(bf16[514,128]{1,0:T(8,128)(2,1)S(1)} %pad_maximum_fusion), channel_id=1, source_target_pairs={{0,8},{8,16},{16,24},{24,32},{32,40},{40,48},{48,56},{56,64},{64,7... | collective-permute-start | bytes 394760 | tf_op jit(solution)/shard_map/ppermute | solution.py:18
  25.2 1.2 copy.31
  26.4 0.8 fusion.49
  27.2 0.8 slice_compare_fusion
  28.1 0.9 fusion.61
  29.0 1.3 copy.48
  30.3 1.3 copy.49
  31.8 0.9 slice.153
  32.7 0.9 slice.154
  33.6 0.9 slice.155
  37.4 0.9 constant_dynamic-update-slice_fusion
  38.3 1.6 select_reduce_fusion
  40.7 1.5 fusion.30
  42.2 1.1 compare_and_fusion
  43.3 3.0 %fusion.25 = (bf16[1280,1,64]{2,0,1:T(8,128)(2,1)S(1)}, bf16[1280,1,64]{2,0,1:T(8,128)(2,1)S(1)}) fusion(f32[1280,1,128]{2,0,1:T(8,128)S(1)} %fusion.37, f32[64]{0:T(128)S(1)} %negate_power_fusion, f32[1280]{0:T(1024)S(1)} %convert_subtract_fusion), kind=kLoop, calls=%fused_computation.30 | loop fusion | flops 737280 | bytes 988416 | tf_op jit(solution)/shard_map/convert.22
  46.3 1.9 fusion.2
  48.2 1.9 fusion
  50.1 2.5 %fusion.13 = bf16[256,1,7,128]{0,3,2,1:T(8,128)(2,1)S(1)} fusion(f32[1280,256,7]{1,0,2:T(8,128)S(1)} %get-tuple-element.23, f32[7,256]{1,0:T(8,128)S(1)} %get-tuple-element.22, pred[256,1280]{0,1:T(8,128)(4,1)S(1)} %compare_and_fusion, f32[256,7]{0,1:T(8,128)S(1)} %bitcast.149, bf16[2,1280,128]{2,1,0:T(8,128)(2,1)S(1)} %constant_dynamic-update-slice_fusion), kind=kOutput, calls=%fused_computation.15 | convolution fusion | flops 596836352 | bytes 10305536 | tf_op jit(solution)/shard_map/hgqk,khd->qhgd/dot_general | solution.py:131
  52.8 1.3 convolution_convert_fusion
  54.1 1.9 collective-permute-start.4
  56.1 1.3 collective-permute-done.4
  57.6 2.4 %collective-permute-start.5 = (bf16[32,1793]{1,0:T(8,128)(2,1)S(1)}, bf16[32,1793]{1,0:T(8,128)(2,1)S(1)}, u32[]{:S(2)}, u32[]{:S(2)}) collective-permute-start(bf16[32,1793]{1,0:T(8,128)(2,1)S(1)} %broadcast_select_fusion.4), channel_id=1, source_target_pairs={{0,16},{8,24},{16,0},{24,8},{32,48},{40,56},{48,32},{56,40},{64,80... | collective-permute-start | bytes 344264 | tf_op jit(solution)/shard_map/ppermute | solution.py:25
  60.0 4.9 %collective-permute-done.5 = bf16[32,1793]{1,0:T(8,128)(2,1)S(1)} collective-permute-done((bf16[32,1793]{1,0:T(8,128)(2,1)S(1)}, bf16[32,1793]{1,0:T(8,128)(2,1)S(1)}, u32[]{:S(2)}, u32[]{:S(2)}) %collective-permute-start.5) | collective-permute-done | bytes 114784 | tf_op jit(solution)/shard_map/ppermute | solution.py:25
  65.1 4.1 %collective-permute-start.6 = (bf16[32,1793]{1,0:T(8,128)(2,1)S(1)}, bf16[32,1793]{1,0:T(8,128)(2,1)S(1)}, u32[]{:S(2)}, u32[]{:S(2)}) collective-permute-start(bf16[32,1793]{1,0:T(8,128)(2,1)S(1)} %broadcast_select_fusion.3), channel_id=1, source_target_pairs={{0,32},{8,40},{16,48},{24,56},{32,0},{40,8},{48,16},{56,24},{64,96... | collective-permute-start | bytes 344264 | tf_op jit(solution)/shard_map/ppermute | solution.py:25
  69.2 4.2 %collective-permute-done.6 = bf16[32,1793]{1,0:T(8,128)(2,1)S(1)} collective-permute-done((bf16[32,1793]{1,0:T(8,128)(2,1)S(1)}, bf16[32,1793]{1,0:T(8,128)(2,1)S(1)}, u32[]{:S(2)}, u32[]{:S(2)}) %collective-permute-start.6) | collective-permute-done | bytes 114784 | tf_op jit(solution)/shard_map/ppermute | solution.py:25
  73.6 4.6 %collective-permute-start.7 = (bf16[32,1793]{1,0:T(8,128)(2,1)S(1)}, bf16[32,1793]{1,0:T(8,128)(2,1)S(1)}, u32[]{:S(2)}, u32[]{:S(2)}) collective-permute-start(bf16[32,1793]{1,0:T(8,128)(2,1)S(1)} %broadcast_select_fusion.2), channel_id=1, source_target_pairs={{0,64},{8,72},{16,80},{24,88},{32,96},{40,104},{48,112},{56,120},{... | collective-permute-start | bytes 344264 | tf_op jit(solution)/shard_map/ppermute | solution.py:25
  78.2 5.2 %collective-permute-done.7 = bf16[32,1793]{1,0:T(8,128)(2,1)S(1)} collective-permute-done((bf16[32,1793]{1,0:T(8,128)(2,1)S(1)}, bf16[32,1793]{1,0:T(8,128)(2,1)S(1)}, u32[]{:S(2)}, u32[]{:S(2)}) %collective-permute-start.7) | collective-permute-done | bytes 114784 | tf_op jit(solution)/shard_map/ppermute | solution.py:25
  83.6 7.3 %collective-permute-start.8 = (bf16[32,1793]{1,0:T(8,128)(2,1)S(1)}, bf16[32,1793]{1,0:T(8,128)(2,1)S(1)}, u32[]{:S(2)}, u32[]{:S(2)}) collective-permute-start(bf16[32,1793]{1,0:T(8,128)(2,1)S(1)} %broadcast_select_fusion.1), channel_id=1, source_target_pairs={{0,128},{8,136},{16,144},{24,152},{32,160},{40,168},{48,176},{56,1... | collective-permute-start | bytes 344264 | tf_op jit(solution)/shard_map/ppermute | solution.py:25
  90.9 7.8 %collective-permute-done.8 = bf16[32,1793]{1,0:T(8,128)(2,1)S(1)} collective-permute-done((bf16[32,1793]{1,0:T(8,128)(2,1)S(1)}, bf16[32,1793]{1,0:T(8,128)(2,1)S(1)}, u32[]{:S(2)}, u32[]{:S(2)}) %collective-permute-start.8) | collective-permute-done | bytes 114784 | tf_op jit(solution)/shard_map/ppermute | solution.py:25
  98.9 6.5 %collective-permute-start.9 = (bf16[32,1793]{1,0:T(8,128)(2,1)S(1)}, bf16[32,1793]{1,0:T(8,128)(2,1)S(1)}, u32[]{:S(2)}, u32[]{:S(2)}) collective-permute-start(bf16[32,1793]{1,0:T(8,128)(2,1)S(1)} %broadcast_select_fusion), channel_id=1, source_target_pairs={{0,256},{8,264},{16,272},{24,280},{32,288},{40,296},{48,304},{56,3... | collective-permute-start | bytes 344264 | tf_op jit(solution)/shard_map/ppermute | solution.py:25
  105.4 8.2 %collective-permute-done.9 = bf16[32,1793]{1,0:T(8,128)(2,1)S(1)} collective-permute-done((bf16[32,1793]{1,0:T(8,128)(2,1)S(1)}, bf16[32,1793]{1,0:T(8,128)(2,1)S(1)}, u32[]{:S(2)}, u32[]{:S(2)}) %collective-permute-start.9) | collective-permute-done | bytes 114784 | tf_op jit(solution)/shard_map/ppermute | solution.py:25
  113.8 1.0 copy.39
  114.8 7.7 %all-gather.2.cloned.1.call-done = bf16[896,7168]{0,1:T(8,128)(2,1)} async-done(((bf16[896,112]{0,1:T(8,128)(2,1)}), bf16[896,7168]{0,1:T(8,128)(2,1)}) %all-gather.2.cloned.1.call-update) | async-done | bytes 12845072 | tf_op jit(solution)/shard_map/all_gather | solution.py:157
  122.5 11.2 %convert_bitcast_fusion = bf16[8,288,896]{2,1,0:T(8,128)(2,1)} fusion(bf16[896,8,896]{0,2,1:T(8,128)(2,1)} %bitcast.151, bf16[32,896]{1,0:T(8,128)(2,1)S(1)} %slice.145, bf16[256,896]{1,0:T(8,128)(2,1)} %copy.39), kind=kOutput, calls=%fused_computation.9 | convolution fusion | flops 3702472704 | bytes 17489920 | tf_op jit(solution)/shard_map/tk,kgn->gtn/dot_general | solution.py:159
  133.7 1.1 slice.182
  134.8 3.2 %collective-permute-start.10 = (bf16[32,4,896]{2,0,1:T(8,128)(2,1)S(1)}, bf16[32,4,896]{2,0,1:T(8,128)(2,1)S(1)}, u32[]{:S(2)}, u32[]{:S(2)}) collective-permute-start(bf16[32,4,896]{2,0,1:T(8,128)(2,1)S(1)} %dynamic-slice_bitcast_fusion), channel_id=1, source_target_pairs={{0,1},{1,0},{2,3},{3,2},{4,5},{5,4},{6,7},{7,6},{8,9},{9,8},{10,11... | collective-permute-start | bytes 688136 | tf_op jit(solution)/shard_map/ppermute | solution.py:42
  138.0 6.4 %collective-permute-done.10 = bf16[32,4,896]{2,0,1:T(8,128)(2,1)S(1)} collective-permute-done((bf16[32,4,896]{2,0,1:T(8,128)(2,1)S(1)}, bf16[32,4,896]{2,0,1:T(8,128)(2,1)S(1)}, u32[]{:S(2)}, u32[]{:S(2)}) %collective-permute-start.10) | collective-permute-done | bytes 229408 | tf_op jit(solution)/shard_map/ppermute | solution.py:42
  144.5 3.9 %collective-permute-start.11 = (bf16[32,2,896]{2,0,1:T(8,128)(2,1)S(1)}, bf16[32,2,896]{2,0,1:T(8,128)(2,1)S(1)}, u32[]{:S(2)}, u32[]{:S(2)}) collective-permute-start(bf16[32,2,896]{2,0,1:T(8,128)(2,1)S(1)} %dynamic-slice_bitcast_fusion.1), channel_id=1, source_target_pairs={{0,2},{1,3},{2,0},{3,1},{4,6},{5,7},{6,4},{7,5},{8,10},{9,11},{10,... | collective-permute-start | bytes 344072 | tf_op jit(solution)/shard_map/ppermute | solution.py:42
  148.5 5.8 %collective-permute-done.11 = bf16[32,2,896]{2,0,1:T(8,128)(2,1)S(1)} collective-permute-done((bf16[32,2,896]{2,0,1:T(8,128)(2,1)S(1)}, bf16[32,2,896]{2,0,1:T(8,128)(2,1)S(1)}, u32[]{:S(2)}, u32[]{:S(2)}) %collective-permute-start.11) | collective-permute-done | bytes 114720 | tf_op jit(solution)/shard_map/ppermute | solution.py:42
  154.3 4.1 %collective-permute-start.12 = (bf16[32,1,896]{2,0,1:T(8,128)(2,1)S(1)}, bf16[32,1,896]{2,0,1:T(8,128)(2,1)S(1)}, u32[]{:S(2)}, u32[]{:S(2)}) collective-permute-start(bf16[32,1,896]{2,0,1:T(8,128)(2,1)S(1)} %constant_dynamic-slice_fusion), channel_id=1, source_target_pairs={{0,4},{1,5},{2,6},{3,7},{4,0},{5,1},{6,2},{7,3},{8,12},{9,13},{10,... | collective-permute-start | bytes 172040 | tf_op jit(solution)/shard_map/ppermute | solution.py:42
  158.5 5.9 %collective-permute-done.12 = bf16[32,1,896]{2,0,1:T(8,128)(2,1)S(1)} collective-permute-done((bf16[32,1,896]{2,0,1:T(8,128)(2,1)S(1)}, bf16[32,1,896]{2,0,1:T(8,128)(2,1)S(1)}, u32[]{:S(2)}, u32[]{:S(2)}) %collective-permute-start.12) | collective-permute-done | bytes 57376 | tf_op jit(solution)/shard_map/ppermute | solution.py:42
  165.3 1.9 collective-permute-start.13
  167.3 4.2 %collective-permute-done.13 = bf16[32,1001]{1,0:T(8,128)(2,1)S(1)} collective-permute-done((bf16[32,1001]{1,0:T(8,128)(2,1)S(1)}, bf16[32,1001]{1,0:T(8,128)(2,1)S(1)}, u32[]{:S(2)}, u32[]{:S(2)}) %collective-permute-start.13) | collective-permute-done | bytes 64096 | tf_op jit(solution)/shard_map/ppermute | solution.py:25
  171.6 3.3 %collective-permute-start.14 = (bf16[32,1001]{1,0:T(8,128)(2,1)S(1)}, bf16[32,1001]{1,0:T(8,128)(2,1)S(1)}, u32[]{:S(2)}, u32[]{:S(2)}) collective-permute-start(bf16[32,1001]{1,0:T(8,128)(2,1)S(1)} %fusion.64), channel_id=1, source_target_pairs={{0,2},{1,3},{2,0},{3,1},{4,6},{5,7},{6,4},{7,5},{8,10},{9,11},{10,... | collective-permute-start | bytes 192200 | tf_op jit(solution)/shard_map/ppermute | solution.py:25
  174.8 5.0 %collective-permute-done.14 = bf16[32,1001]{1,0:T(8,128)(2,1)S(1)} collective-permute-done((bf16[32,1001]{1,0:T(8,128)(2,1)S(1)}, bf16[32,1001]{1,0:T(8,128)(2,1)S(1)}, u32[]{:S(2)}, u32[]{:S(2)}) %collective-permute-start.14) | collective-permute-done | bytes 64096 | tf_op jit(solution)/shard_map/ppermute | solution.py:25
  179.8 4.4 %collective-permute-start.15 = (bf16[32,1001]{1,0:T(8,128)(2,1)S(1)}, bf16[32,1001]{1,0:T(8,128)(2,1)S(1)}, u32[]{:S(2)}, u32[]{:S(2)}) collective-permute-start(bf16[32,1001]{1,0:T(8,128)(2,1)S(1)} %add.116), channel_id=1, source_target_pairs={{0,4},{1,5},{2,6},{3,7},{4,0},{5,1},{6,2},{7,3},{8,12},{9,13},{10,... | collective-permute-start | bytes 192200 | tf_op jit(solution)/shard_map/ppermute | solution.py:25
  184.2 7.6 %collective-permute-done.15 = bf16[32,1001]{1,0:T(8,128)(2,1)S(1)} collective-permute-done((bf16[32,1001]{1,0:T(8,128)(2,1)S(1)}, bf16[32,1001]{1,0:T(8,128)(2,1)S(1)}, u32[]{:S(2)}, u32[]{:S(2)}) %collective-permute-start.15) | collective-permute-done | bytes 64096 | tf_op jit(solution)/shard_map/ppermute | solution.py:25
  192.8 1.9 collective-permute-start.16
  194.7 1.1 collective-permute-done.16
  195.8 2.6 %collective-permute-start.17 = (f32[32]{0:T(128)S(1)}, f32[32]{0:T(128)S(1)}, u32[]{:S(2)}, u32[]{:S(2)}) collective-permute-start(f32[32]{0:T(128)S(1)} %max.18), channel_id=1, source_target_pairs={{0,16},{8,24},{16,0},{24,8},{32,48},{40,56},{48,32},{56,40},{64,80... | collective-permute-start | bytes 392 | tf_op jit(solution)/shard_map/ppermute | solution.py:25
  198.4 2.8 %collective-permute-done.17 = f32[32]{0:T(128)S(1)} collective-permute-done((f32[32]{0:T(128)S(1)}, f32[32]{0:T(128)S(1)}, u32[]{:S(2)}, u32[]{:S(2)}) %collective-permute-start.17) | collective-permute-done | bytes 160 | tf_op jit(solution)/shard_map/ppermute | solution.py:25
  201.2 3.2 %collective-permute-start.18 = (f32[32]{0:T(128)S(1)}, f32[32]{0:T(128)S(1)}, u32[]{:S(2)}, u32[]{:S(2)}) collective-permute-start(f32[32]{0:T(128)S(1)} %max.19), channel_id=1, source_target_pairs={{0,32},{8,40},{16,48},{24,56},{32,0},{40,8},{48,16},{56,24},{64,96... | collective-permute-start | bytes 392 | tf_op jit(solution)/shard_map/ppermute | solution.py:25
  204.4 3.7 %collective-permute-done.18 = f32[32]{0:T(128)S(1)} collective-permute-done((f32[32]{0:T(128)S(1)}, f32[32]{0:T(128)S(1)}, u32[]{:S(2)}, u32[]{:S(2)}) %collective-permute-start.18) | collective-permute-done | bytes 160 | tf_op jit(solution)/shard_map/ppermute | solution.py:25
  208.1 1.9 collective-permute-start.19
  210.1 3.5 %collective-permute-done.19 = f32[32]{0:T(128)S(1)} collective-permute-done((f32[32]{0:T(128)S(1)}, f32[32]{0:T(128)S(1)}, u32[]{:S(2)}, u32[]{:S(2)}) %collective-permute-start.19) | collective-permute-done | bytes 160 | tf_op jit(solution)/shard_map/ppermute | solution.py:25
  213.6 2.0 collective-permute-start.20
  215.6 4.3 %collective-permute-done.20 = f32[32]{0:T(128)S(1)} collective-permute-done((f32[32]{0:T(128)S(1)}, f32[32]{0:T(128)S(1)}, u32[]{:S(2)}, u32[]{:S(2)}) %collective-permute-start.20) | collective-permute-done | bytes 160 | tf_op jit(solution)/shard_map/ppermute | solution.py:25
  219.9 4.9 %collective-permute-start.21 = (f32[32]{0:T(128)S(1)}, f32[32]{0:T(128)S(1)}, u32[]{:S(2)}, u32[]{:S(2)}) collective-permute-start(f32[32]{0:T(128)S(1)} %max.22), channel_id=1, source_target_pairs={{0,256},{8,264},{16,272},{24,280},{32,288},{40,296},{48,304},{56,3... | collective-permute-start | bytes 392 | tf_op jit(solution)/shard_map/ppermute | solution.py:25
  225.6 3.7 %collective-permute-done.21 = f32[32]{0:T(128)S(1)} collective-permute-done((f32[32]{0:T(128)S(1)}, f32[32]{0:T(128)S(1)}, u32[]{:S(2)}, u32[]{:S(2)}) %collective-permute-start.21) | collective-permute-done | bytes 160 | tf_op jit(solution)/shard_map/ppermute | solution.py:25
  229.7 2.0 fusion.19
  (76 shorter events, 10.2 us)
Async XLA Ops:
  7.2 157.4 %copy-start = (bf16[896,1000]{0,1:T(8,128)(2,1)S(1)}, bf16[896,1000]{0,1:T(8,128)(2,1)}, u32[]{:S(2)}) copy-start(bf16[896,1000]{0,1:T(8,128)(2,1)} %param.13) | copy-start | bytes 5376004
  7.2 35.0 %copy-start.1 = (s32[256]{0:T(256)S(1)}, s32[256]{0:T(256)}, u32[]{:S(2)}) copy-start(s32[256]{0:T(256)} %param.9) | copy-start | bytes 3076
  7.2 115.3 %all-gather.2.cloned.1.call-start = ((), (), s32[]{:S(2)}) async-start(), calls=%async_computation.1 | async-start | bytes 13045760 | tf_op jit(solution)/shard_map/all_gather | solution.py:157
  7.9 221.8 %reduce-scatter.2.cloned.1.call-start = ((), (), s32[]{:S(2)}) async-start(), calls=%async_computation.2 | async-start | bytes 4644864 | tf_op jit(solution)/shard_map/reduce_scatter | solution.py:168
  9.6 22.2 %collective-permute-start = (bf16[514,128]{1,0:T(8,128)(2,1)S(1)}, bf16[514,128]{1,0:T(8,128)(2,1)S(1)}, u32[]{:S(2)}, u32[]{:S(2)}) collective-permute-start(bf16[514,128]{1,0:T(8,128)(2,1)S(1)} %pad_maximum_fusion), channel_id=1, source_target_pairs={{0,32},{8,40},{16,48},{24,56},{32,64},{40,72},{48,80},{56,88},{64,... | collective-permute-start | bytes 394760 | tf_op jit(solution)/shard_map/ppermute | solution.py:18
  14.5 17.3 %collective-permute-start.1 = (bf16[514,128]{1,0:T(8,128)(2,1)S(1)}, bf16[514,128]{1,0:T(8,128)(2,1)}, u32[]{:S(2)}, u32[]{:S(2)}) collective-permute-start(bf16[514,128]{1,0:T(8,128)(2,1)S(1)} %pad_maximum_fusion), channel_id=1, source_target_pairs={{0,24},{8,32},{16,40},{24,48},{32,56},{40,64},{48,72},{56,80},{64,... | collective-permute-start | bytes 394760 | tf_op jit(solution)/shard_map/ppermute | solution.py:18
  16.8 15.9 %collective-permute-start.2 = (bf16[514,128]{1,0:T(8,128)(2,1)S(1)}, bf16[514,128]{1,0:T(8,128)(2,1)}, u32[]{:S(2)}, u32[]{:S(2)}) collective-permute-start(bf16[514,128]{1,0:T(8,128)(2,1)S(1)} %pad_maximum_fusion), channel_id=1, source_target_pairs={{0,16},{8,24},{16,32},{24,40},{32,48},{40,56},{48,64},{56,72},{64,... | collective-permute-start | bytes 394760 | tf_op jit(solution)/shard_map/ppermute | solution.py:18
  21.1 12.6 %collective-permute-start.3 = (bf16[514,128]{1,0:T(8,128)(2,1)S(1)}, bf16[514,128]{1,0:T(8,128)(2,1)}, u32[]{:S(2)}, u32[]{:S(2)}) collective-permute-start(bf16[514,128]{1,0:T(8,128)(2,1)S(1)} %pad_maximum_fusion), channel_id=1, source_target_pairs={{0,8},{8,16},{16,24},{24,32},{32,40},{40,48},{48,56},{56,64},{64,7... | collective-permute-start | bytes 394760 | tf_op jit(solution)/shard_map/ppermute | solution.py:18
  54.1 3.2 %collective-permute-start.4 = (bf16[32,1793]{1,0:T(8,128)(2,1)S(1)}, bf16[32,1793]{1,0:T(8,128)(2,1)S(1)}, u32[]{:S(2)}, u32[]{:S(2)}) collective-permute-start(bf16[32,1793]{1,0:T(8,128)(2,1)S(1)} %pad_maximum_fusion.1), channel_id=1, source_target_pairs={{0,8},{8,0},{16,24},{24,16},{32,40},{40,32},{48,56},{56,48},{64,72... | collective-permute-start | bytes 344264 | tf_op jit(solution)/shard_map/ppermute | solution.py:25
  57.6 7.3 %collective-permute-start.5 = (bf16[32,1793]{1,0:T(8,128)(2,1)S(1)}, bf16[32,1793]{1,0:T(8,128)(2,1)S(1)}, u32[]{:S(2)}, u32[]{:S(2)}) collective-permute-start(bf16[32,1793]{1,0:T(8,128)(2,1)S(1)} %broadcast_select_fusion.4), channel_id=1, source_target_pairs={{0,16},{8,24},{16,0},{24,8},{32,48},{40,56},{48,32},{56,40},{64,80... | collective-permute-start | bytes 344264 | tf_op jit(solution)/shard_map/ppermute | solution.py:25
  65.1 8.3 %collective-permute-start.6 = (bf16[32,1793]{1,0:T(8,128)(2,1)S(1)}, bf16[32,1793]{1,0:T(8,128)(2,1)S(1)}, u32[]{:S(2)}, u32[]{:S(2)}) collective-permute-start(bf16[32,1793]{1,0:T(8,128)(2,1)S(1)} %broadcast_select_fusion.3), channel_id=1, source_target_pairs={{0,32},{8,40},{16,48},{24,56},{32,0},{40,8},{48,16},{56,24},{64,96... | collective-permute-start | bytes 344264 | tf_op jit(solution)/shard_map/ppermute | solution.py:25
  73.6 9.8 %collective-permute-start.7 = (bf16[32,1793]{1,0:T(8,128)(2,1)S(1)}, bf16[32,1793]{1,0:T(8,128)(2,1)S(1)}, u32[]{:S(2)}, u32[]{:S(2)}) collective-permute-start(bf16[32,1793]{1,0:T(8,128)(2,1)S(1)} %broadcast_select_fusion.2), channel_id=1, source_target_pairs={{0,64},{8,72},{16,80},{24,88},{32,96},{40,104},{48,112},{56,120},{... | collective-permute-start | bytes 344264 | tf_op jit(solution)/shard_map/ppermute | solution.py:25
  83.6 15.1 %collective-permute-start.8 = (bf16[32,1793]{1,0:T(8,128)(2,1)S(1)}, bf16[32,1793]{1,0:T(8,128)(2,1)S(1)}, u32[]{:S(2)}, u32[]{:S(2)}) collective-permute-start(bf16[32,1793]{1,0:T(8,128)(2,1)S(1)} %broadcast_select_fusion.1), channel_id=1, source_target_pairs={{0,128},{8,136},{16,144},{24,152},{32,160},{40,168},{48,176},{56,1... | collective-permute-start | bytes 344264 | tf_op jit(solution)/shard_map/ppermute | solution.py:25
  98.9 14.7 %collective-permute-start.9 = (bf16[32,1793]{1,0:T(8,128)(2,1)S(1)}, bf16[32,1793]{1,0:T(8,128)(2,1)S(1)}, u32[]{:S(2)}, u32[]{:S(2)}) collective-permute-start(bf16[32,1793]{1,0:T(8,128)(2,1)S(1)} %broadcast_select_fusion), channel_id=1, source_target_pairs={{0,256},{8,264},{16,272},{24,280},{32,288},{40,296},{48,304},{56,3... | collective-permute-start | bytes 344264 | tf_op jit(solution)/shard_map/ppermute | solution.py:25
  122.5 41.9 %copy-start.2 = (bf16[896]{0:T(1024)(128)(2,1)S(1)}, bf16[896]{0:T(1024)(128)(2,1)}, u32[]{:S(2)}) copy-start(bf16[896]{0:T(1024)(128)(2,1)} %param.12) | copy-start | bytes 5380
  134.8 9.7 %collective-permute-start.10 = (bf16[32,4,896]{2,0,1:T(8,128)(2,1)S(1)}, bf16[32,4,896]{2,0,1:T(8,128)(2,1)S(1)}, u32[]{:S(2)}, u32[]{:S(2)}) collective-permute-start(bf16[32,4,896]{2,0,1:T(8,128)(2,1)S(1)} %dynamic-slice_bitcast_fusion), channel_id=1, source_target_pairs={{0,1},{1,0},{2,3},{3,2},{4,5},{5,4},{6,7},{7,6},{8,9},{9,8},{10,11... | collective-permute-start | bytes 688136 | tf_op jit(solution)/shard_map/ppermute | solution.py:42
  144.5 9.7 %collective-permute-start.11 = (bf16[32,2,896]{2,0,1:T(8,128)(2,1)S(1)}, bf16[32,2,896]{2,0,1:T(8,128)(2,1)S(1)}, u32[]{:S(2)}, u32[]{:S(2)}) collective-permute-start(bf16[32,2,896]{2,0,1:T(8,128)(2,1)S(1)} %dynamic-slice_bitcast_fusion.1), channel_id=1, source_target_pairs={{0,2},{1,3},{2,0},{3,1},{4,6},{5,7},{6,4},{7,5},{8,10},{9,11},{10,... | collective-permute-start | bytes 344072 | tf_op jit(solution)/shard_map/ppermute | solution.py:42
  154.3 10.0 %collective-permute-start.12 = (bf16[32,1,896]{2,0,1:T(8,128)(2,1)S(1)}, bf16[32,1,896]{2,0,1:T(8,128)(2,1)S(1)}, u32[]{:S(2)}, u32[]{:S(2)}) collective-permute-start(bf16[32,1,896]{2,0,1:T(8,128)(2,1)S(1)} %constant_dynamic-slice_fusion), channel_id=1, source_target_pairs={{0,4},{1,5},{2,6},{3,7},{4,0},{5,1},{6,2},{7,3},{8,12},{9,13},{10,... | collective-permute-start | bytes 172040 | tf_op jit(solution)/shard_map/ppermute | solution.py:42
  165.3 6.2 %collective-permute-start.13 = (bf16[32,1001]{1,0:T(8,128)(2,1)S(1)}, bf16[32,1001]{1,0:T(8,128)(2,1)S(1)}, u32[]{:S(2)}, u32[]{:S(2)}) collective-permute-start(bf16[32,1001]{1,0:T(8,128)(2,1)S(1)} %pad_maximum_fusion.3), channel_id=1, source_target_pairs={{0,1},{1,0},{2,3},{3,2},{4,5},{5,4},{6,7},{7,6},{8,9},{9,8},{10,11... | collective-permute-start | bytes 192200 | tf_op jit(solution)/shard_map/ppermute | solution.py:25
  171.6 8.2 %collective-permute-start.14 = (bf16[32,1001]{1,0:T(8,128)(2,1)S(1)}, bf16[32,1001]{1,0:T(8,128)(2,1)S(1)}, u32[]{:S(2)}, u32[]{:S(2)}) collective-permute-start(bf16[32,1001]{1,0:T(8,128)(2,1)S(1)} %fusion.64), channel_id=1, source_target_pairs={{0,2},{1,3},{2,0},{3,1},{4,6},{5,7},{6,4},{7,5},{8,10},{9,11},{10,... | collective-permute-start | bytes 192200 | tf_op jit(solution)/shard_map/ppermute | solution.py:25
  179.8 12.0 %collective-permute-start.15 = (bf16[32,1001]{1,0:T(8,128)(2,1)S(1)}, bf16[32,1001]{1,0:T(8,128)(2,1)S(1)}, u32[]{:S(2)}, u32[]{:S(2)}) collective-permute-start(bf16[32,1001]{1,0:T(8,128)(2,1)S(1)} %add.116), channel_id=1, source_target_pairs={{0,4},{1,5},{2,6},{3,7},{4,0},{5,1},{6,2},{7,3},{8,12},{9,13},{10,... | collective-permute-start | bytes 192200 | tf_op jit(solution)/shard_map/ppermute | solution.py:25
  192.8 3.0 %collective-permute-start.16 = (f32[32]{0:T(128)S(1)}, f32[32]{0:T(128)S(1)}, u32[]{:S(2)}, u32[]{:S(2)}) collective-permute-start(f32[32]{0:T(128)S(1)} %fusion.41), channel_id=1, source_target_pairs={{0,8},{8,0},{16,24},{24,16},{32,40},{40,32},{48,56},{56,48},{64,72... | collective-permute-start | bytes 392 | tf_op jit(solution)/shard_map/ppermute | solution.py:25
  195.8 5.4 %collective-permute-start.17 = (f32[32]{0:T(128)S(1)}, f32[32]{0:T(128)S(1)}, u32[]{:S(2)}, u32[]{:S(2)}) collective-permute-start(f32[32]{0:T(128)S(1)} %max.18), channel_id=1, source_target_pairs={{0,16},{8,24},{16,0},{24,8},{32,48},{40,56},{48,32},{56,40},{64,80... | collective-permute-start | bytes 392 | tf_op jit(solution)/shard_map/ppermute | solution.py:25
  201.2 6.9 %collective-permute-start.18 = (f32[32]{0:T(128)S(1)}, f32[32]{0:T(128)S(1)}, u32[]{:S(2)}, u32[]{:S(2)}) collective-permute-start(f32[32]{0:T(128)S(1)} %max.19), channel_id=1, source_target_pairs={{0,32},{8,40},{16,48},{24,56},{32,0},{40,8},{48,16},{56,24},{64,96... | collective-permute-start | bytes 392 | tf_op jit(solution)/shard_map/ppermute | solution.py:25
  208.1 5.4 %collective-permute-start.19 = (f32[32]{0:T(128)S(1)}, f32[32]{0:T(128)S(1)}, u32[]{:S(2)}, u32[]{:S(2)}) collective-permute-start(f32[32]{0:T(128)S(1)} %max.20), channel_id=1, source_target_pairs={{0,64},{8,72},{16,80},{24,88},{32,96},{40,104},{48,112},{56,120},{... | collective-permute-start | bytes 392 | tf_op jit(solution)/shard_map/ppermute | solution.py:25
  213.6 6.3 %collective-permute-start.20 = (f32[32]{0:T(128)S(1)}, f32[32]{0:T(128)S(1)}, u32[]{:S(2)}, u32[]{:S(2)}) collective-permute-start(f32[32]{0:T(128)S(1)} %max.21), channel_id=1, source_target_pairs={{0,128},{8,136},{16,144},{24,152},{32,160},{40,168},{48,176},{56,1... | collective-permute-start | bytes 392 | tf_op jit(solution)/shard_map/ppermute | solution.py:25
  219.9 9.3 %collective-permute-start.21 = (f32[32]{0:T(128)S(1)}, f32[32]{0:T(128)S(1)}, u32[]{:S(2)}, u32[]{:S(2)}) collective-permute-start(f32[32]{0:T(128)S(1)} %max.22), channel_id=1, source_target_pairs={{0,256},{8,264},{16,272},{24,280},{32,288},{40,296},{48,304},{56,3... | collective-permute-start | bytes 392 | tf_op jit(solution)/shard_map/ppermute | solution.py:25
Sparse Core Ops, SparseCore 0:
  11.3 111.1 all-gather.1
  164.5 56.8 reduce-scatter.1
where the time goes:
time: 240 us; the launch traced here: 239 us
  waiting for transfers between devices  93.8 us (39%)
  starting transfers between devices  79.9 us (33%)
  other arithmetic  20.6 us (9%)
  matrix products  17.5 us (7%)
  between operations  14.6 us (6%)
  local copies, waits for them, and re-layouts  12.2 us (5%)
    ppermute x15, waiting for transfers between devices, butterfly(): lax.ppermute(value, axis, [(source, source ^ stride) for source in range(...  67.4 us
    ppermute x15, starting transfers between devices, butterfly(): lax.ppermute(value, axis, [(source, source ^ stride) for source in range(...  53 us
    ppermute x3, waiting for transfers between devices, halving_scatter(): lax.ppermute(give, axis, [(source, source ^ bit) for source in range(coun...  18 us
    ppermute x4, starting transfers between devices, from_behind(): lax.ppermute(value, axis, [(source, source + steps) for source in range(i...  15.6 us
    ppermute x3, starting transfers between devices, halving_scatter(): lax.ppermute(give, axis, [(source, source ^ bit) for source in range(coun...  11.2 us
    dot_general x1, matrix products, local(): jnp.einsum('tk,kgn->gtn', jnp.concatenate([attended, end_att], axis=0), f...  11.2 us
    all_gather x1, waiting for transfers between devices, local(): full_weight = lax.all_gather(out_weight, 'req', axis=1, tiled=True)  7.7 us
  transfers between devices with their start and end apart: 24, of which 19 were waited for; matrix products, arithmetic and copies ran while one was open for 15% of the time, Pallas kernels for 0%

commit v1 on v0

--- a/solution.py
+++ b/solution.py
@@ -154,7 +154,10 @@
     end_rows = butterfly(end_rows, "req", latest)[:, :-1]
     attended, end_rows = lax.optimization_barrier((attended, end_rows))
     end_att, end_res = (end_rows[:, : attended.shape[1]], end_rows[:, attended.shape[1] :])
-    full_weight = lax.all_gather(out_weight, "req", axis=1, tiled=True)
+    size = lax.axis_size("req")
+    tiles = jnp.stack([out_weight for _ in range(size)])
+    tiles = lax.all_to_all(tiles, "req", split_axis=0, concat_axis=0)
+    full_weight = jnp.concatenate(tiles, axis=1)
     groups = lax.axis_size("tp")
     both = jnp.einsum(
         "tk,kgn->gtn",

time: 240 us -> 505 us (2.10)
  starting transfers between devices: 79.9 us -> 335 us
  waiting for transfers between devices: 93.8 us -> 99.5 us
    ppermute x15, starting transfers between devices: 53 us -> 294 us  [butterfly(): lax.ppermute(value, axis, [(source, source ^ stride) for source in range(...]
    ppermute x4, waiting for transfers between devices: 0.01 us -> 31.8 us  [from_behind(): lax.ppermute(value, axis, [(source, source + steps) for source in range(i...]
    ppermute x15, waiting for transfers between devices: 67.4 us -> 52.2 us  [butterfly(): lax.ppermute(value, axis, [(source, source ^ stride) for source in range(...]
    all_to_all x0 -> x1, starting transfers between devices: none -> 14.1 us  [local(): tiles = lax.all_to_all(tiles, 'req', split_axis=0, concat_axis=0)]
    all_gather x1 -> x0, waiting for transfers between devices: 7.7 us -> none  [local(): full_weight = lax.all_gather(out_weight, 'req', axis=1, tiled=True)]
    another operation x0 -> x1, local copies, waits for them, and re-layouts: none -> 6.6 us  [local(): tiles = jnp.stack([out_weight for _ in range(size)])]
  transfers between devices with their start and end apart: 24 -> 24, of which waited for: 19 -> 21; matrix products, arithmetic and copies ran while one was open for 15% -> 6% of each run, Pallas kernels for 0% -> 0%
where the time goes in v1:
time: 505 us; the launch traced here: 502 us
  starting transfers between devices  335 us (66%)
  waiting for transfers between devices  99.5 us (20%)
  other arithmetic  18.2 us (4%)
  matrix products  17.5 us (3%)
  local copies, waits for them, and re-layouts  17.1 us (3%)
  between operations  14.6 us (3%)
    ppermute x15, starting transfers between devices, butterfly(): lax.ppermute(value, axis, [(source, source ^ stride) for source in range(...  294 us
    ppermute x15, waiting for transfers between devices, butterfly(): lax.ppermute(value, axis, [(source, source ^ stride) for source in range(...  52.2 us
    ppermute x4, waiting for transfers between devices, from_behind(): lax.ppermute(value, axis, [(source, source + steps) for source in range(i...  31.8 us
    ppermute x3, waiting for transfers between devices, halving_scatter(): lax.ppermute(give, axis, [(source, source ^ bit) for source in range(coun...  15.5 us
    ppermute x4, starting transfers between devices, from_behind(): lax.ppermute(value, axis, [(source, source + steps) for source in range(i...  14.7 us
    all_to_all x1, starting transfers between devices, local(): tiles = lax.all_to_all(tiles, 'req', split_axis=0, concat_axis=0)  14.1 us
    ppermute x3, starting transfers between devices, halving_scatter(): lax.ppermute(give, axis, [(source, source ^ bit) for source in range(coun...  11.9 us
    dot_general x1, matrix products, local(): jnp.einsum('tk,kgn->gtn', jnp.concatenate([attended, end_att], axis=0), f...  11.2 us
  transfers between devices with their start and end apart: 24, of which 21 were waited for; matrix products, arithmetic and copies ran while one was open for 6% of the time, Pallas kernels for 0%

profile of v1, /device:TPU:56, one launch (start us, length us, event | category | flops | bytes accessed | tf_op | source)
XLA Modules:
  0.0 502.0 jit_solution(5473272313386717117)
XLA Ops:
  7.2 6.6 %stack.2 = bf16[64,896,112]{1,2,0:T(8,128)(2,1)} broadcast(bf16[896,112]{0,1:T(8,128)(2,1)} %param.11), dimensions={1,2} | broadcast | bytes 13045760 | tf_op jit(solution)/shard_map/stack | solution.py:158
  13.8 14.1 %all-to-all-start = ((bf16[64,896,112]{1,2,0:T(8,128)(2,1)}), bf16[64,896,112]{1,2,0:T(8,128)(2,1)}, u32[]{:S(2)}, u32[]{:S(2)}) async-start(bf16[64,896,112]{1,2,0:T(8,128)(2,1)} %stack.2), calls=%async_computation | async-start | bytes 25690112 | tf_op jit(solution)/shard_map/all_to_all | solution.py:159
  28.0 5.6 %collective-permute-start = (bf16[514,128]{1,0:T(8,128)(2,1)S(1)}, bf16[514,128]{1,0:T(8,128)(2,1)}, u32[]{:S(2)}, u32[]{:S(2)}) collective-permute-start(bf16[514,128]{1,0:T(8,128)(2,1)S(1)} %pad_maximum_fusion), channel_id=1, source_target_pairs={{0,32},{8,40},{16,48},{24,56},{32,64},{40,72},{48,80},{56,88},{64,... | collective-permute-start | bytes 394760 | tf_op jit(solution)/shard_map/ppermute | solution.py:18
  33.6 2.6 collective-permute-start.1
  36.2 2.8 collective-permute-start.2
  39.0 3.8 collective-permute-start.3
  43.2 0.9 fusion.61
  44.2 1.3 copy.50
  45.5 1.3 copy.49
  46.9 18.1 %collective-permute-done = bf16[514,128]{1,0:T(8,128)(2,1)} collective-permute-done((bf16[514,128]{1,0:T(8,128)(2,1)S(1)}, bf16[514,128]{1,0:T(8,128)(2,1)}, u32[]{:S(2)}, u32[]{:S(2)}) %collective-permute-start) | collective-permute-done | bytes 131616 | tf_op jit(solution)/shard_map/ppermute | solution.py:18
  65.0 0.9 slice.152
  65.9 10.9 %collective-permute-done.1 = bf16[514,128]{1,0:T(8,128)(2,1)} collective-permute-done((bf16[514,128]{1,0:T(8,128)(2,1)S(1)}, bf16[514,128]{1,0:T(8,128)(2,1)}, u32[]{:S(2)}, u32[]{:S(2)}) %collective-permute-start.1) | collective-permute-done | bytes 131616 | tf_op jit(solution)/shard_map/ppermute | solution.py:18
  76.8 0.9 slice.153
  77.7 2.8 collective-permute-done.2
  80.5 0.9 slice.154
  81.5 0.9 slice.155
  85.2 1.6 select_reduce_fusion
  87.5 1.5 fusion.30
  89.0 1.1 compare_and_fusion
  90.2 3.0 fusion.25
  93.2 1.9 fusion.2
  95.1 1.9 fusion
  97.0 2.5 fusion.13
  99.7 1.3 convolution_convert_fusion
  101.0 2.0 collective-permute-start.4
  103.0 1.2 collective-permute-done.4
  104.5 4.5 collective-permute-start.5
  109.0 5.8 %collective-permute-done.5 = bf16[32,1793]{1,0:T(8,128)(2,1)S(1)} collective-permute-done((bf16[32,1793]{1,0:T(8,128)(2,1)S(1)}, bf16[32,1793]{1,0:T(8,128)(2,1)S(1)}, u32[]{:S(2)}, u32[]{:S(2)}) %collective-permute-start.5) | collective-permute-done | bytes 114784 | tf_op jit(solution)/shard_map/ppermute | solution.py:25
  115.0 235.8 %collective-permute-start.6 = (bf16[32,1793]{1,0:T(8,128)(2,1)S(1)}, bf16[32,1793]{1,0:T(8,128)(2,1)S(1)}, u32[]{:S(2)}, u32[]{:S(2)}) collective-permute-start(bf16[32,1793]{1,0:T(8,128)(2,1)S(1)} %broadcast_select_fusion.3), channel_id=1, source_target_pairs={{0,32},{8,40},{16,48},{24,56},{32,0},{40,8},{48,16},{56,24},{64,96... | collective-permute-start | bytes 344264 | tf_op jit(solution)/shard_map/ppermute | solution.py:25
  350.8 3.1 collective-permute-done.6
  354.2 7.5 %collective-permute-start.7 = (bf16[32,1793]{1,0:T(8,128)(2,1)S(1)}, bf16[32,1793]{1,0:T(8,128)(2,1)S(1)}, u32[]{:S(2)}, u32[]{:S(2)}) collective-permute-start(bf16[32,1793]{1,0:T(8,128)(2,1)S(1)} %broadcast_select_fusion.2), channel_id=1, source_target_pairs={{0,64},{8,72},{16,80},{24,88},{32,96},{40,104},{48,112},{56,120},{... | collective-permute-start | bytes 344264 | tf_op jit(solution)/shard_map/ppermute | solution.py:25
  361.6 2.8 collective-permute-done.7
  364.7 5.3 %collective-permute-start.8 = (bf16[32,1793]{1,0:T(8,128)(2,1)S(1)}, bf16[32,1793]{1,0:T(8,128)(2,1)S(1)}, u32[]{:S(2)}, u32[]{:S(2)}) collective-permute-start(bf16[32,1793]{1,0:T(8,128)(2,1)S(1)} %broadcast_select_fusion.1), channel_id=1, source_target_pairs={{0,128},{8,136},{16,144},{24,152},{32,160},{40,168},{48,176},{56,1... | collective-permute-start | bytes 344264 | tf_op jit(solution)/shard_map/ppermute | solution.py:25
  370.0 2.9 collective-permute-done.8
  373.0 6.2 %collective-permute-start.9 = (bf16[32,1793]{1,0:T(8,128)(2,1)S(1)}, bf16[32,1793]{1,0:T(8,128)(2,1)S(1)}, u32[]{:S(2)}, u32[]{:S(2)}) collective-permute-start(bf16[32,1793]{1,0:T(8,128)(2,1)S(1)} %broadcast_select_fusion), channel_id=1, source_target_pairs={{0,256},{8,264},{16,272},{24,280},{32,288},{40,296},{48,304},{56,3... | collective-permute-start | bytes 344264 | tf_op jit(solution)/shard_map/ppermute | solution.py:25
  379.3 5.0 %collective-permute-done.9 = bf16[32,1793]{1,0:T(8,128)(2,1)S(1)} collective-permute-done((bf16[32,1793]{1,0:T(8,128)(2,1)S(1)}, bf16[32,1793]{1,0:T(8,128)(2,1)S(1)}, u32[]{:S(2)}, u32[]{:S(2)}) %collective-permute-start.9) | collective-permute-done | bytes 114784 | tf_op jit(solution)/shard_map/ppermute | solution.py:25
  384.6 1.0 copy.40
  385.6 11.2 %convert_bitcast_fusion = bf16[8,288,896]{2,1,0:T(8,128)(2,1)} fusion(bf16[896,8,896]{0,2,1:T(8,128)(2,1)} %bitcast.33, bf16[32,896]{1,0:T(8,128)(2,1)S(1)} %slice.145, bf16[256,896]{1,0:T(8,128)(2,1)} %copy.40), kind=kOutput, calls=%fused_computation.9 | convolution fusion | flops 3702472704 | bytes 17489920 | tf_op jit(solution)/shard_map/tk,kgn->gtn/dot_general | solution.py:162
  396.8 1.1 slice.182
  397.9 3.2 collective-permute-start.10
  401.2 4.6 collective-permute-done.10
  405.9 4.6 collective-permute-start.11
  410.5 4.8 collective-permute-done.11
  415.4 4.1 collective-permute-start.12
  419.5 6.0 %collective-permute-done.12 = bf16[32,1,896]{2,0,1:T(8,128)(2,1)S(1)} collective-permute-done((bf16[32,1,896]{2,0,1:T(8,128)(2,1)S(1)}, bf16[32,1,896]{2,0,1:T(8,128)(2,1)S(1)}, u32[]{:S(2)}, u32[]{:S(2)}) %collective-permute-start.12) | collective-permute-done | bytes 57376 | tf_op jit(solution)/shard_map/ppermute | solution.py:42
  426.5 2.1 collective-permute-start.13
  428.6 4.1 collective-permute-done.13
  432.7 3.2 collective-permute-start.14
  436.0 4.6 collective-permute-done.14
  440.6 5.1 %collective-permute-start.15 = (bf16[32,1001]{1,0:T(8,128)(2,1)S(1)}, bf16[32,1001]{1,0:T(8,128)(2,1)S(1)}, u32[]{:S(2)}, u32[]{:S(2)}) collective-permute-start(bf16[32,1001]{1,0:T(8,128)(2,1)S(1)} %add.116), channel_id=1, source_target_pairs={{0,4},{1,5},{2,6},{3,7},{4,0},{5,1},{6,2},{7,3},{8,12},{9,13},{10,... | collective-permute-start | bytes 192200 | tf_op jit(solution)/shard_map/ppermute | solution.py:25
  445.7 6.8 %collective-permute-done.15 = bf16[32,1001]{1,0:T(8,128)(2,1)S(1)} collective-permute-done((bf16[32,1001]{1,0:T(8,128)(2,1)S(1)}, bf16[32,1001]{1,0:T(8,128)(2,1)S(1)}, u32[]{:S(2)}, u32[]{:S(2)}) %collective-permute-start.15) | collective-permute-done | bytes 64096 | tf_op jit(solution)/shard_map/ppermute | solution.py:25
  453.4 1.9 collective-permute-start.16
  455.3 1.1 collective-permute-done.16
  456.4 2.7 collective-permute-start.17
  459.2 2.7 collective-permute-done.17
  461.9 2.3 collective-permute-start.18
  464.2 4.6 collective-permute-done.18
  468.8 3.6 collective-permute-start.19
  472.4 1.8 collective-permute-done.19
  474.2 7.5 %collective-permute-start.20 = (f32[32]{0:T(128)S(1)}, f32[32]{0:T(128)S(1)}, u32[]{:S(2)}, u32[]{:S(2)}) collective-permute-start(f32[32]{0:T(128)S(1)} %max.21), channel_id=1, source_target_pairs={{0,128},{8,136},{16,144},{24,152},{32,160},{40,168},{48,176},{56,1... | collective-permute-start | bytes 392 | tf_op jit(solution)/shard_map/ppermute | solution.py:25
  481.8 1.5 collective-permute-done.20
  483.3 4.4 collective-permute-start.21
  488.4 4.2 collective-permute-done.21
  493.1 2.0 fusion.19
  (80 shorter events, 9.1 us)
Async XLA Ops:
  7.2 418.6 %copy-start = (bf16[896,1000]{0,1:T(8,128)(2,1)S(1)}, bf16[896,1000]{0,1:T(8,128)(2,1)}, u32[]{:S(2)}) copy-start(bf16[896,1000]{0,1:T(8,128)(2,1)} %param.13) | copy-start | bytes 5376004
  13.8 14.2 %copy-start.3 = (s32[256]{0:T(256)S(1)}, s32[256]{0:T(256)}, u32[]{:S(2)}) copy-start(s32[256]{0:T(256)} %param.9) | copy-start | bytes 3076
  13.8 14.2 %copy-start.1 = (bf16[2,256,128]{2,1,0:T(8,128)(2,1)S(1)}, bf16[2,256,128]{2,1,0:T(8,128)(2,1)}, u32[]{:S(2)}) copy-start(bf16[2,256,128]{2,1,0:T(8,128)(2,1)} %param.8) | copy-start | bytes 393220
  13.8 29.0 %copy-start.2 = (bf16[256,896]{1,0:T(8,128)(2,1)S(1)}, bf16[256,896]{1,0:T(8,128)(2,1)}, u32[]{:S(2)}) copy-start(bf16[256,896]{1,0:T(8,128)(2,1)} %param.7) | copy-start | bytes 1376260
  13.8 371.8 %all-to-all-start = ((bf16[64,896,112]{1,2,0:T(8,128)(2,1)}), bf16[64,896,112]{1,2,0:T(8,128)(2,1)}, u32[]{:S(2)}, u32[]{:S(2)}) async-start(bf16[64,896,112]{1,2,0:T(8,128)(2,1)} %stack.2), calls=%async_computation | async-start | bytes 25690112 | tf_op jit(solution)/shard_map/all_to_all | solution.py:159
  27.9 465.2 %reduce-scatter.2.cloned.1.call-start = ((), (), s32[]{:S(2)}) async-start(), calls=%async_computation.2 | async-start | bytes 4644864 | tf_op jit(solution)/shard_map/reduce_scatter | solution.py:171
  28.0 36.9 %collective-permute-start = (bf16[514,128]{1,0:T(8,128)(2,1)S(1)}, bf16[514,128]{1,0:T(8,128)(2,1)}, u32[]{:S(2)}, u32[]{:S(2)}) collective-permute-start(bf16[514,128]{1,0:T(8,128)(2,1)S(1)} %pad_maximum_fusion), channel_id=1, source_target_pairs={{0,32},{8,40},{16,48},{24,56},{32,64},{40,72},{48,80},{56,88},{64,... | collective-permute-start | bytes 394760 | tf_op jit(solution)/shard_map/ppermute | solution.py:18
  33.6 43.2 %collective-permute-start.1 = (bf16[514,128]{1,0:T(8,128)(2,1)S(1)}, bf16[514,128]{1,0:T(8,128)(2,1)}, u32[]{:S(2)}, u32[]{:S(2)}) collective-permute-start(bf16[514,128]{1,0:T(8,128)(2,1)S(1)} %pad_maximum_fusion), channel_id=1, source_target_pairs={{0,24},{8,32},{16,40},{24,48},{32,56},{40,64},{48,72},{56,80},{64,... | collective-permute-start | bytes 394760 | tf_op jit(solution)/shard_map/ppermute | solution.py:18
  36.2 44.3 %collective-permute-start.2 = (bf16[514,128]{1,0:T(8,128)(2,1)S(1)}, bf16[514,128]{1,0:T(8,128)(2,1)}, u32[]{:S(2)}, u32[]{:S(2)}) collective-permute-start(bf16[514,128]{1,0:T(8,128)(2,1)S(1)} %pad_maximum_fusion), channel_id=1, source_target_pairs={{0,16},{8,24},{16,32},{24,40},{32,48},{40,56},{48,64},{56,72},{64,... | collective-permute-start | bytes 394760 | tf_op jit(solution)/shard_map/ppermute | solution.py:18
  39.0 42.5 %collective-permute-start.3 = (bf16[514,128]{1,0:T(8,128)(2,1)S(1)}, bf16[514,128]{1,0:T(8,128)(2,1)}, u32[]{:S(2)}, u32[]{:S(2)}) collective-permute-start(bf16[514,128]{1,0:T(8,128)(2,1)S(1)} %pad_maximum_fusion), channel_id=1, source_target_pairs={{0,8},{8,16},{16,24},{24,32},{32,40},{40,48},{48,56},{56,64},{64,7... | collective-permute-start | bytes 394760 | tf_op jit(solution)/shard_map/ppermute | solution.py:18
  101.0 3.2 collective-permute-start.4
  104.5 10.3 %collective-permute-start.5 = (bf16[32,1793]{1,0:T(8,128)(2,1)S(1)}, bf16[32,1793]{1,0:T(8,128)(2,1)S(1)}, u32[]{:S(2)}, u32[]{:S(2)}) collective-permute-start(bf16[32,1793]{1,0:T(8,128)(2,1)S(1)} %broadcast_select_fusion.4), channel_id=1, source_target_pairs={{0,16},{8,24},{16,0},{24,8},{32,48},{40,56},{48,32},{56,40},{64,80... | collective-permute-start | bytes 344264 | tf_op jit(solution)/shard_map/ppermute | solution.py:25
  115.0 239.0 %collective-permute-start.6 = (bf16[32,1793]{1,0:T(8,128)(2,1)S(1)}, bf16[32,1793]{1,0:T(8,128)(2,1)S(1)}, u32[]{:S(2)}, u32[]{:S(2)}) collective-permute-start(bf16[32,1793]{1,0:T(8,128)(2,1)S(1)} %broadcast_select_fusion.3), channel_id=1, source_target_pairs={{0,32},{8,40},{16,48},{24,56},{32,0},{40,8},{48,16},{56,24},{64,96... | collective-permute-start | bytes 344264 | tf_op jit(solution)/shard_map/ppermute | solution.py:25
  354.2 10.3 %collective-permute-start.7 = (bf16[32,1793]{1,0:T(8,128)(2,1)S(1)}, bf16[32,1793]{1,0:T(8,128)(2,1)S(1)}, u32[]{:S(2)}, u32[]{:S(2)}) collective-permute-start(bf16[32,1793]{1,0:T(8,128)(2,1)S(1)} %broadcast_select_fusion.2), channel_id=1, source_target_pairs={{0,64},{8,72},{16,80},{24,88},{32,96},{40,104},{48,112},{56,120},{... | collective-permute-start | bytes 344264 | tf_op jit(solution)/shard_map/ppermute | solution.py:25
  364.7 8.1 %collective-permute-start.8 = (bf16[32,1793]{1,0:T(8,128)(2,1)S(1)}, bf16[32,1793]{1,0:T(8,128)(2,1)S(1)}, u32[]{:S(2)}, u32[]{:S(2)}) collective-permute-start(bf16[32,1793]{1,0:T(8,128)(2,1)S(1)} %broadcast_select_fusion.1), channel_id=1, source_target_pairs={{0,128},{8,136},{16,144},{24,152},{32,160},{40,168},{48,176},{56,1... | collective-permute-start | bytes 344264 | tf_op jit(solution)/shard_map/ppermute | solution.py:25
  373.0 11.3 %collective-permute-start.9 = (bf16[32,1793]{1,0:T(8,128)(2,1)S(1)}, bf16[32,1793]{1,0:T(8,128)(2,1)S(1)}, u32[]{:S(2)}, u32[]{:S(2)}) collective-permute-start(bf16[32,1793]{1,0:T(8,128)(2,1)S(1)} %broadcast_select_fusion), channel_id=1, source_target_pairs={{0,256},{8,264},{16,272},{24,280},{32,288},{40,296},{48,304},{56,3... | collective-permute-start | bytes 344264 | tf_op jit(solution)/shard_map/ppermute | solution.py:25
  385.6 40.0 %copy-start.4 = (bf16[896]{0:T(1024)(128)(2,1)S(1)}, bf16[896]{0:T(1024)(128)(2,1)}, u32[]{:S(2)}) copy-start(bf16[896]{0:T(1024)(128)(2,1)} %param.12) | copy-start | bytes 5380
  397.9 7.9 %collective-permute-start.10 = (bf16[32,4,896]{2,0,1:T(8,128)(2,1)S(1)}, bf16[32,4,896]{2,0,1:T(8,128)(2,1)S(1)}, u32[]{:S(2)}, u32[]{:S(2)}) collective-permute-start(bf16[32,4,896]{2,0,1:T(8,128)(2,1)S(1)} %dynamic-slice_bitcast_fusion), channel_id=1, source_target_pairs={{0,1},{1,0},{2,3},{3,2},{4,5},{5,4},{6,7},{7,6},{8,9},{9,8},{10,11... | collective-permute-start | bytes 688136 | tf_op jit(solution)/shard_map/ppermute | solution.py:42
  405.9 9.4 %collective-permute-start.11 = (bf16[32,2,896]{2,0,1:T(8,128)(2,1)S(1)}, bf16[32,2,896]{2,0,1:T(8,128)(2,1)S(1)}, u32[]{:S(2)}, u32[]{:S(2)}) collective-permute-start(bf16[32,2,896]{2,0,1:T(8,128)(2,1)S(1)} %dynamic-slice_bitcast_fusion.1), channel_id=1, source_target_pairs={{0,2},{1,3},{2,0},{3,1},{4,6},{5,7},{6,4},{7,5},{8,10},{9,11},{10,... | collective-permute-start | bytes 344072 | tf_op jit(solution)/shard_map/ppermute | solution.py:42
  415.4 10.1 %collective-permute-start.12 = (bf16[32,1,896]{2,0,1:T(8,128)(2,1)S(1)}, bf16[32,1,896]{2,0,1:T(8,128)(2,1)S(1)}, u32[]{:S(2)}, u32[]{:S(2)}) collective-permute-start(bf16[32,1,896]{2,0,1:T(8,128)(2,1)S(1)} %constant_dynamic-slice_fusion), channel_id=1, source_target_pairs={{0,4},{1,5},{2,6},{3,7},{4,0},{5,1},{6,2},{7,3},{8,12},{9,13},{10,... | collective-permute-start | bytes 172040 | tf_op jit(solution)/shard_map/ppermute | solution.py:42
  426.5 6.2 %collective-permute-start.13 = (bf16[32,1001]{1,0:T(8,128)(2,1)S(1)}, bf16[32,1001]{1,0:T(8,128)(2,1)S(1)}, u32[]{:S(2)}, u32[]{:S(2)}) collective-permute-start(bf16[32,1001]{1,0:T(8,128)(2,1)S(1)} %pad_maximum_fusion.3), channel_id=1, source_target_pairs={{0,1},{1,0},{2,3},{3,2},{4,5},{5,4},{6,7},{7,6},{8,9},{9,8},{10,11... | collective-permute-start | bytes 192200 | tf_op jit(solution)/shard_map/ppermute | solution.py:25
  432.7 7.8 %collective-permute-start.14 = (bf16[32,1001]{1,0:T(8,128)(2,1)S(1)}, bf16[32,1001]{1,0:T(8,128)(2,1)S(1)}, u32[]{:S(2)}, u32[]{:S(2)}) collective-permute-start(bf16[32,1001]{1,0:T(8,128)(2,1)S(1)} %fusion.64), channel_id=1, source_target_pairs={{0,2},{1,3},{2,0},{3,1},{4,6},{5,7},{6,4},{7,5},{8,10},{9,11},{10,... | collective-permute-start | bytes 192200 | tf_op jit(solution)/shard_map/ppermute | solution.py:25
  440.6 11.9 %collective-permute-start.15 = (bf16[32,1001]{1,0:T(8,128)(2,1)S(1)}, bf16[32,1001]{1,0:T(8,128)(2,1)S(1)}, u32[]{:S(2)}, u32[]{:S(2)}) collective-permute-start(bf16[32,1001]{1,0:T(8,128)(2,1)S(1)} %add.116), channel_id=1, source_target_pairs={{0,4},{1,5},{2,6},{3,7},{4,0},{5,1},{6,2},{7,3},{8,12},{9,13},{10,... | collective-permute-start | bytes 192200 | tf_op jit(solution)/shard_map/ppermute | solution.py:25
  453.4 3.0 collective-permute-start.16
  456.4 5.4 %collective-permute-start.17 = (f32[32]{0:T(128)S(1)}, f32[32]{0:T(128)S(1)}, u32[]{:S(2)}, u32[]{:S(2)}) collective-permute-start(f32[32]{0:T(128)S(1)} %max.18), channel_id=1, source_target_pairs={{0,16},{8,24},{16,0},{24,8},{32,48},{40,56},{48,32},{56,40},{64,80... | collective-permute-start | bytes 392 | tf_op jit(solution)/shard_map/ppermute | solution.py:25
  461.9 6.9 %collective-permute-start.18 = (f32[32]{0:T(128)S(1)}, f32[32]{0:T(128)S(1)}, u32[]{:S(2)}, u32[]{:S(2)}) collective-permute-start(f32[32]{0:T(128)S(1)} %max.19), channel_id=1, source_target_pairs={{0,32},{8,40},{16,48},{24,56},{32,0},{40,8},{48,16},{56,24},{64,96... | collective-permute-start | bytes 392 | tf_op jit(solution)/shard_map/ppermute | solution.py:25
  468.8 5.4 %collective-permute-start.19 = (f32[32]{0:T(128)S(1)}, f32[32]{0:T(128)S(1)}, u32[]{:S(2)}, u32[]{:S(2)}) collective-permute-start(f32[32]{0:T(128)S(1)} %max.20), channel_id=1, source_target_pairs={{0,64},{8,72},{16,80},{24,88},{32,96},{40,104},{48,112},{56,120},{... | collective-permute-start | bytes 392 | tf_op jit(solution)/shard_map/ppermute | solution.py:25
  474.2 9.1 %collective-permute-start.20 = (f32[32]{0:T(128)S(1)}, f32[32]{0:T(128)S(1)}, u32[]{:S(2)}, u32[]{:S(2)}) collective-permute-start(f32[32]{0:T(128)S(1)} %max.21), channel_id=1, source_target_pairs={{0,128},{8,136},{16,144},{24,152},{32,160},{40,168},{48,176},{56,1... | collective-permute-start | bytes 392 | tf_op jit(solution)/shard_map/ppermute | solution.py:25
  483.3 9.3 %collective-permute-start.21 = (f32[32]{0:T(128)S(1)}, f32[32]{0:T(128)S(1)}, u32[]{:S(2)}, u32[]{:S(2)}) collective-permute-start(f32[32]{0:T(128)S(1)} %max.22), channel_id=1, source_target_pairs={{0,256},{8,264},{16,272},{24,280},{32,288},{40,296},{48,304},{56,3... | collective-permute-start | bytes 392 | tf_op jit(solution)/shard_map/ppermute | solution.py:25
Sparse Core Ops, SparseCore 0:
  425.6 56.7 reduce-scatter.1
